TPU v7x, 32 devices: a whole 2x2x4 slice. The times are simulated.
32 devices in a mesh: grp: 2 (over y), seq: 16 (over z, x, core).
Axes of the slice: x: 2, y: 2, z: 4, core: 2. Of those that a mesh axis runs over, the one named last changes fastest.
Arguments:
- ssm_in: bfloat16 [2048, 4096], P(('grp', 'seq')), parts along dimension 0
- ssm_dt: bfloat16 [2048, 4096], P(('grp', 'seq')), parts along dimension 0, as said below
- ssm_a: float32 [16, 4096], replicated, as said below
- ssm_b: float32 [16, 2048], P(None, ('grp', 'seq')), parts along dimension 1, may hold values from -0.1875 to 0.1875
- ssm_c: float32 [16, 2048], P(None, ('grp', 'seq')), parts along dimension 1, may hold values from -1.5 to 1.5
- attn_q: bfloat16 [2048, 4096], P(('grp', 'seq')), parts along dimension 0
- attn_kv: bfloat16 [2048, 2048], P(('grp', 'seq')), parts along dimension 0
- moe_in: bfloat16 [2048, 4096], P(('grp', 'seq')), parts along dimension 0, may hold values from -6 to 6
- moe_routes: int32 [2048, 2], P(('grp', 'seq')), parts along dimension 0, may hold values from 0 to 15, all different within a row; in each aligned block of 64 rows (0 to 63, 64 to 127, ...) at most 12 rows name the same one
- moe_prob: float32 [2048, 2], P(('grp', 'seq')), parts along dimension 0, may hold values from 0.2 to 1
- w_gate: bfloat16 [4096, 4096], P(None, 'seq'), may hold values from -0.09375 to 0.09375
- w_up: bfloat16 [4096, 4096], P(None, 'seq'), may hold values from -0.09375 to 0.09375
- w_down: bfloat16 [4096, 4096], P('seq'), may hold values from -0.1875 to 0.1875
Outputs:
- ssm_out: bfloat16 [2048, 4096], P(('grp', 'seq')), parts along dimension 0
- attn_out: bfloat16 [2048, 4096], P(('grp', 'seq')), parts along dimension 0
- moe_out: bfloat16 [2048, 4096], P(('grp', 'seq')), parts along dimension 0
There are 2 independent parts, one for each index of `grp`. A program takes and returns all parts, laid end to end along the dimension named above; an argument that names none is the same for every part. Nothing has to cross between parts.
Inputs may be any that keep to these rules, and one draw needn't show every extreme that they name: `moe_routes`: no expert is named by more than 12 positions of one device; a position's two experts differ. `ssm_dt`: Positive. `ssm_a`: Negative.
All inputs are finite; a program needn't handle non-finite values.
Results may differ from a plain program's by a relative error of at most 0.0079.
Values may be sent and summed in bfloat16 or wider, within the bound.
No kernel may reach another device: no remote copies, remote signals or barrier semaphores. Data moves between devices by JAX's collectives and lax.ppermute only.
A program may use at most 192 MiB of HBM per device.

v0:
```python
import math
import jax
import jax.numpy as jnp
from jax import lax
from jax.sharding import PartitionSpec as P

HQ = 32
HK = 8
HEAD_SIZE = 128
EXP_WIN = 4
CAP = 12


def prefix(value, axis, join, neutral):
    count, mine = (lax.axis_size(axis), lax.axis_index(axis))
    pieces = jax.tree.map(lambda part: lax.all_gather(part, axis), value)
    running = jax.tree.map(
        lambda part, zero: jnp.full_like(part, 0) + jnp.asarray(zero, part.dtype), value, neutral
    )

    def hop(position, running):
        longer = join(running, jax.tree.map(lambda part: part[position], pieces))
        return jax.tree.map(lambda new, old: jnp.where(position < mine, new, old), longer, running)

    return lax.fori_loop(0, count - 1, hop, running)


def shifted(value, axis, by):
    devices = lax.axis_size(axis)
    pairs = [(i, i + by) for i in range(devices) if 0 <= i + by < devices]
    return lax.ppermute(value, axis, pairs)


def sweep(initial, values, deltas, rates, inject_rows, read_rows):

    def advance(carried, packet):
        value_row, delta_row, inject_row, read_row = packet
        carried = (
            jnp.exp(delta_row[None, :] * rates) * carried
            + (delta_row * value_row)[None, :] * inject_row[:, None]
        )
        return (carried, jnp.sum(read_row[:, None] * carried, axis=0))

    return lax.scan(advance, initial, (values, deltas, inject_rows.T, read_rows.T), unroll=8)


def ssm_correct(local_read, local_end, deltas, rates, read_rows):
    mine = lax.axis_index("seq")
    running = jnp.cumsum(deltas, axis=0)
    ends = lax.all_gather(local_end, "seq")
    sums = lax.all_gather(running[-1], "seq")
    devices = sums.shape[0]
    order = jnp.arange(devices, dtype=jnp.int32)
    masked = jnp.where((order < mine)[:, None], sums, 0.0)
    after = jnp.sum(masked, axis=0)[None, :] - jnp.cumsum(masked, axis=0)
    after = jnp.maximum(after, 0.0)
    carry = jnp.exp(rates[None] * after[:, None, :]) * ends
    incoming = jnp.sum(jnp.where((order < mine)[:, None, None], carry, 0.0), axis=0)
    growth = jnp.exp(rates[None] * running[:, None, :]) * incoming[None]
    fix = jnp.sum(read_rows.T[:, :, None] * growth, axis=1)
    return (local_read + fix).astype(jnp.bfloat16)


def chain_join(earlier, later):
    return (earlier[0] * later[0], later[0] * earlier[1] + later[1])


def attend(queries, window, query_pos, key_pos):
    count = queries.shape[0]
    key_count = window.shape[0]
    repeat = HQ // HK
    query_head_tensor = queries.reshape(count, HK, repeat, HEAD_SIZE)
    key_head_tensor = window[:, : HK * HEAD_SIZE].reshape(key_count, HK, HEAD_SIZE)
    value_head_tensor = window[:, HK * HEAD_SIZE :].reshape(key_count, HK, HEAD_SIZE)
    attention_scores = jnp.einsum(
        "bajq,oaq->ajbo", query_head_tensor, key_head_tensor, preferred_element_type=jnp.float32
    ) / math.sqrt(HEAD_SIZE)
    allowed = (key_pos[None, :] >= 0) & (key_pos[None, :] <= query_pos[:, None])
    attention_scores = jnp.where(allowed[None, None], attention_scores, -jnp.inf)
    row_max = jnp.max(attention_scores, axis=-1, keepdims=True)
    expd = jnp.exp(attention_scores - row_max)
    probabilities = (expd / jnp.sum(expd, axis=-1, keepdims=True)).astype(jnp.bfloat16)
    expert_mixture = jnp.einsum(
        "kyje,eku->jkyu", probabilities, value_head_tensor, preferred_element_type=jnp.float32
    )
    return expert_mixture.reshape(count, HQ * HEAD_SIZE).astype(jnp.bfloat16)


def expert_partial(gathered, w_gate, w_up, w_down):
    gate_pre = jnp.dot(gathered, w_gate, preferred_element_type=jnp.float32)
    up_pre = jnp.dot(gathered, w_up, preferred_element_type=jnp.float32)
    hidden_act = (jax.nn.silu(gate_pre) * up_pre).astype(jnp.bfloat16)
    return jnp.dot(hidden_act, w_down, preferred_element_type=jnp.float32).astype(jnp.bfloat16)


def body(
    ssm_in,
    ssm_dt,
    ssm_a,
    ssm_b,
    ssm_c,
    attn_q,
    attn_kv,
    moe_in,
    moe_routes,
    moe_prob,
    w_gate,
    w_up,
    w_down,
):
    values = ssm_in.astype(jnp.float32)
    deltas = ssm_dt.astype(jnp.float32)
    initial = jnp.zeros(ssm_a.shape, jnp.float32)
    local_end, local_read = sweep(initial, values, deltas, ssm_a, ssm_b, ssm_c)
    ssm_out = ssm_correct(local_read, local_end, deltas, ssm_a, ssm_c)
    count = attn_q.shape[0]
    block_index = lax.axis_index("seq")
    one_back = shifted(attn_kv, "seq", 1)
    two_back = shifted(attn_kv, "seq", 2)
    window = jnp.concatenate([two_back, one_back, attn_kv], axis=0)
    first_row = block_index * count
    query_pos = first_row + jnp.arange(count, dtype=jnp.int32)
    key_pos = first_row - 2 * count + jnp.arange(3 * count, dtype=jnp.int32)
    attn_out = attend(attn_q, window, query_pos, key_pos)
    stream = (
        moe_in.astype(jnp.float32) + ssm_out.astype(jnp.float32) + attn_out.astype(jnp.float32)
    ).astype(jnp.bfloat16)
    local_tokens = stream.shape[0]
    width = stream.shape[1]
    seq_count = lax.axis_size("seq")
    group = seq_count // EXP_WIN
    expert_ids = jnp.arange(EXP_WIN, dtype=jnp.int32)
    matches = moe_routes[:, :, None] == expert_ids[None, None, :]
    routed = jnp.any(matches, axis=1).astype(jnp.int32)
    route_share = jnp.sum(jnp.where(matches, moe_prob[:, :, None], 0.0), axis=1)
    position_rank = jnp.cumsum(routed, axis=0) - 1
    picker = (routed[:, :, None] == 1) & (
        position_rank[:, :, None] == jnp.arange(CAP, dtype=jnp.int32)[None, None, :]
    )
    packed = jnp.einsum(
        "tek,td->ekd", picker.astype(jnp.bfloat16), stream, preferred_element_type=jnp.float32
    ).astype(jnp.bfloat16)
    outgoing = jnp.repeat(packed, group, axis=0)
    arrived = lax.all_to_all(outgoing, "seq", split_axis=0, concat_axis=0, tiled=True)
    gathered = arrived.reshape(-1, arrived.shape[-1])
    partial_value = expert_partial(gathered, w_gate, w_up, w_down)
    returned = lax.all_to_all(
        partial_value.reshape(arrived.shape), "seq", split_axis=0, concat_axis=0, tiled=True
    )
    summed = jnp.sum(returned.reshape(EXP_WIN, group, CAP, width), axis=1, dtype=jnp.float32)
    weighting = (picker.astype(jnp.float32) * route_share[:, :, None]).reshape(
        local_tokens, EXP_WIN * CAP
    )
    combined = jnp.dot(
        weighting,
        summed.reshape(EXP_WIN * CAP, width),
        precision=lax.Precision.HIGHEST,
        preferred_element_type=jnp.float32,
    )
    moe_out = combined.astype(jnp.bfloat16)
    return (ssm_out, attn_out, moe_out)


def solution(mesh):
    return jax.shard_map(
        body,
        mesh=mesh,
        in_specs=(
            P(("grp", "seq"), None),
            P(("grp", "seq"), None),
            P(),
            P(None, ("grp", "seq")),
            P(None, ("grp", "seq")),
            P(("grp", "seq"), None),
            P(("grp", "seq"), None),
            P(("grp", "seq"), None),
            P(("grp", "seq"), None),
            P(("grp", "seq"), None),
            P(None, "seq"),
            P(None, "seq"),
            P("seq", None),
        ),
        out_specs=(P(("grp", "seq"), None), P(("grp", "seq"), None), P(("grp", "seq"), None)),
        check_vma=False,
    )
```

profile of v0, /device:TPU:11, one launch (start us, length us, event | category | flops | bytes accessed | tf_op | source)
XLA Modules:
  0.0 243.2 jit_solution(3421550089307953260)
XLA Ops:
  7.3 2.2 convert_bitcast_fusion
  9.5 2.1 bitcast_convert_fusion
  11.9 37.0 %while.13 = (s32[]{:T(128)}, f32[16,4096]{1,0:T(8,128)S(1)}, f32[8,8,4096]{2,1,0:T(8,128)}, f32[8,8,4096]{2,1,0:T(8,128)}, f32[16,4096]{1,0:T(8,128)S(1)}, /*ind...) while((s32[]{:T(128)}, f32[16,4096]{1,0:T(8,128)S(1)}, ...), condition=%wide.region_9.10_spmd.clone, body=%wide.region_0.9_spmd.clone.sunk | while | flops 4587530 | bytes 5150316 | solution.py:44
  11.9 2.1 constant_dynamic-slice_fusion.21
  16.2 2.6 %constant_dynamic-slice_fusion.21 = (f32[1,1,4096]{2,1,0:T(1,128)S(1)}, f32[1,1,4096]{2,1,0:T(1,128)S(1)}, f32[1,1,4096]{2,1,0:T(1,128)S(1)}, f32[1,1,4096]{2,1,...) fusion(f32[8,8,4096]{2,1,0:T(8,128)} %get-tuple-element.330, ...), kind=kLoop, calls=%fused_computation.24.clone.1 | loop fusion | bytes 524320 | tf_op jit(solution)/shard_map/while/body/slice | solution.py:44
  21.1 2.3 constant_dynamic-slice_fusion.21
  25.6 2.3 constant_dynamic-slice_fusion.21
  30.2 2.6 %constant_dynamic-slice_fusion.21 = (f32[1,1,4096]{2,1,0:T(1,128)S(1)}, f32[1,1,4096]{2,1,0:T(1,128)S(1)}, f32[1,1,4096]{2,1,0:T(1,128)S(1)}, f32[1,1,4096]{2,1,...) fusion(f32[8,8,4096]{2,1,0:T(8,128)} %get-tuple-element.330, ...), kind=kLoop, calls=%fused_computation.24.clone.1 | loop fusion | bytes 524320 | tf_op jit(solution)/shard_map/while/body/slice | solution.py:44
  35.0 2.3 constant_dynamic-slice_fusion.21
  39.5 2.4 constant_dynamic-slice_fusion.21
  44.1 2.5 %constant_dynamic-slice_fusion.21 = (f32[1,1,4096]{2,1,0:T(1,128)S(1)}, f32[1,1,4096]{2,1,0:T(1,128)S(1)}, f32[1,1,4096]{2,1,0:T(1,128)S(1)}, f32[1,1,4096]{2,1,...) fusion(f32[8,8,4096]{2,1,0:T(8,128)} %get-tuple-element.330, ...), kind=kLoop, calls=%fused_computation.24.clone.1 | loop fusion | bytes 524320 | tf_op jit(solution)/shard_map/while/body/slice | solution.py:44
  49.6 3.2 %collective-permute-start = (bf16[64,2048]{1,0:T(8,128)(2,1)}, bf16[64,2048]{1,0:T(8,128)(2,1)}, u32[]{:S(2)}, u32[]{:S(2)}) collective-permute-start(bf16[64,2048]{1,0:T(8,128)(2,1)} %param.21), channel_id=1, source_target_pairs={{0,2},{1,3},{2,4},{3,5},{4,6},{5,7},{6,8},{7,9},{8,10},{9,11},{10,... | collective-permute-start | bytes 786440 | tf_op jit(solution)/shard_map/ppermute | solution.py:31
  52.8 4.0 %collective-permute-start.1 = (bf16[64,2048]{1,0:T(8,128)(2,1)}, bf16[64,2048]{1,0:T(8,128)(2,1)}, u32[]{:S(2)}, u32[]{:S(2)}) collective-permute-start(bf16[64,2048]{1,0:T(8,128)(2,1)} %param.21), channel_id=1, source_target_pairs={{0,1},{1,2},{2,3},{3,4},{4,5},{5,6},{6,7},{7,8},{8,9},{9,10},{10,1... | collective-permute-start | bytes 786440 | tf_op jit(solution)/shard_map/ppermute | solution.py:31
  56.7 1.9 reduce_window_sum.33
  59.6 18.1 %all-gather.1 = f32[16,1,4096]{2,1,0:T(1,128)S(1)} all-gather(f32[1,1,4096]{2,1,0:T(1,128)S(1)} %slice_bitcast_fusion.18), channel_id=1, replica_groups=mesh['grp'=2,'seq'=16] {'seq'}, dimensions={0}, use_global_device_ids=true | all-gather | bytes 278528 | tf_op jit(solution)/shard_map/all_gather | solution.py:51
  78.6 1.2 reshape.321
  80.8 1.0 constant_dynamic-update-slice_fusion.1
  84.5 3.3 %fusion.50 = (f32[8,4,64]{2,1,0:T(4,128)S(1)}, f32[8,4,64,192]{3,2,1,0:T(8,128)}) fusion(pred[64,192]{1,0:T(8,128)(4,1)S(1)} %compare_and_fusion, bf16[64,8,4,128]{3,2,1,0:T(4,128)(2,1)S(1)} %copy-done.9, bf16[192,8,128,1]{2,1,0,3:T(8,128)(2,1)} %bitcast.206), kind=kOutput, calls=%fused_computation.119 | convolution fusion | flops 102236352 | bytes 2510848 | tf_op jit(solution)/shard_map/sub | solution.py:81
  87.8 2.2 fusion.4
  90.4 1.2 convert_element_type.67
  91.6 11.2 %all-gather.4.cloned.1.call-done = f32[256,4096]{1,0:T(8,128)} async-done(((f32[16,4096]{1,0:T(8,128)}), f32[256,4096]{1,0:T(8,128)}) %all-gather.4.cloned.1.call-update) | async-done | bytes 4194320 | tf_op jit(solution)/shard_map/all_gather | solution.py:50
  102.8 3.1 %select_reduce_fusion = f32[16,4096]{1,0:T(8,128)S(1)} fusion(f32[16,16,4096]{2,1,0:T(8,128)} %bitcast.183, f32[16,4096]{1,0:T(8,128)S(1)} %subtract_maximum_fusion, f32[16,4096]{1,0:T(8,128)S(1)} %get-tuple-element.343, pred[16]{0:T(512)(128)(4,1)S(1)} %iota_compare_fusion.2), kind=kLoop, calls=%fused_computation.59 | loop fusion | flops 4128768 | bytes 4980752 | tf_op jit(solution)/shard_map/reduce_sum | solution.py:58
  105.9 5.3 %multiply_reduce_fusion.8 = f32[64,4096]{1,0:T(8,128)S(1)} fusion(f32[16,4096]{1,0:T(8,128)S(1)} %select_reduce_fusion, f32[64,4096]{1,0:T(8,128)S(1)} %copy-done.6, f32[16,4096]{1,0:T(8,128)S(1)} %get-tuple-element.343, f32[64,16]{1,0:T(8,128)S(1)} %bitcast.209), kind=kLoop, calls=%fused_computation.53 | loop fusion | flops 16515072 | bytes 2625536 | tf_op jit(solution)/shard_map/reduce_sum | solution.py:60
  113.3 51.8 %all_to_all.10 = bf16[16,12,4096]{2,1,0:T(8,128)(2,1)} all-to-all(bf16[16,12,4096]{2,1,0:T(8,128)(2,1)S(1)} %bitcast.167), channel_id=1, replica_groups=mesh['grp'=2,'seq'=16] {'seq'}, dimensions={0} | all-to-all | bytes 3145728 | tf_op jit(solution)/shard_map/all_to_all | solution.py:144
  165.1 3.6 %reshape.323 = bf16[192,4096]{1,0:T(8,128)(2,1)} reshape(bf16[16,12,4096]{2,1,0:T(8,128)(2,1)} %all_to_all.10) | data formatting | bytes 3145728 | tf_op jit(solution)/shard_map/reshape | solution.py:145
  168.7 2.6 %fusion.55 = f32[192,256]{1,0:T(8,128)S(1)} fusion(bf16[192,4096]{1,0:T(8,128)(2,1)} %reshape.323, bf16[4096,256]{1,0:T(8,128)(2,1)} %param.25), kind=kOutput, calls=%fused_computation.120 | convolution fusion | flops 402653184 | bytes 3866624 | tf_op jit(solution)/shard_map/dot_general | solution.py:90
  171.3 5.1 %convolution_convert_fusion = bf16[192,4096]{1,0:T(8,128)(2,1)} fusion(bf16[256,4096]{1,0:T(8,128)(2,1)S(1)} %copy-done, bf16[192,4096]{1,0:T(8,128)(2,1)} %reshape.323, bf16[4096,256]{1,0:T(8,128)(2,1)} %param.26, f32[192,256]{1,0:T(8,128)S(1)} %fusion.55), kind=kOutput, calls=%fused_computation.54 | convolution fusion | flops 806387712 | bytes 7536640 | tf_op jit(solution)/shard_map/dot_general | solution.py:93
  176.4 3.4 %reshape.324 = bf16[16,12,4096]{2,1,0:T(8,128)(2,1)} reshape(bf16[192,4096]{1,0:T(8,128)(2,1)} %convolution_convert_fusion) | data formatting | bytes 3145728 | tf_op jit(solution)/shard_map/reshape | solution.py:148
  179.9 5.0 %all-to-all-start.1 = ((bf16[16,12,4096]{2,1,0:T(8,128)(2,1)}), bf16[16,12,4096]{2,1,0:T(8,128)(2,1)}, u32[]{:S(2)}, u32[]{:S(2)}) async-start(bf16[16,12,4096]{2,1,0:T(8,128)(2,1)} %reshape.324), calls=%async_computation.1 | async-start | bytes 4194304 | tf_op jit(solution)/shard_map/all_to_all | solution.py:147
  184.9 47.5 %all-to-all-done.1 = bf16[16,12,4096]{2,1,0:T(8,128)(2,1)} async-done(((bf16[16,12,4096]{2,1,0:T(8,128)(2,1)}), bf16[16,12,4096]{2,1,0:T(8,128)(2,1)}, u32[]{:S(2)}, u32[]{:S(2)}) %all-to-all-start.1) | async-done | bytes 1572896 | tf_op jit(solution)/shard_map/all_to_all | solution.py:147
  232.4 2.1 convert_reduce_fusion
  234.5 1.8 fusion.2
  (199 shorter events, 25.7 us)
Async XLA Ops:
  7.2 164.2 %copy-start = (bf16[256,4096]{1,0:T(8,128)(2,1)S(1)}, bf16[256,4096]{1,0:T(8,128)(2,1)}, u32[]{:S(2)}) copy-start(bf16[256,4096]{1,0:T(8,128)(2,1)} %param.27) | copy-start | bytes 6291460
  7.2 4.5 %copy-start.11 = (f32[16,64]{1,0:T(8,128)S(1)}, f32[16,64]{1,0:T(8,128)}, u32[]{:S(2)}) copy-start(f32[16,64]{1,0:T(8,128)} %param.18) | copy-start | bytes 12292
  7.2 4.6 %copy-start.12 = (f32[16,64]{1,0:T(8,128)S(1)}, f32[16,64]{1,0:T(8,128)}, u32[]{:S(2)}) copy-start(f32[16,64]{1,0:T(8,128)} %param.19) | copy-start | bytes 12292
  7.2 4.6 %copy-start.1 = (f32[16,4096]{1,0:T(8,128)S(1)}, f32[16,4096]{1,0:T(8,128)}, u32[]{:S(2)}) copy-start(f32[16,4096]{1,0:T(8,128)} %param.17) | copy-start | bytes 786436
  7.2 95.6 %all-gather.4.cloned.1.call-start = ((), (), s32[]{:S(2)}) async-start(), calls=%async_computation.2 | async-start | bytes 4456448 | tf_op jit(solution)/shard_map/all_gather | solution.py:50
  11.8 44.9 %copy-start.3 = (bf16[64,4096]{1,0:T(8,128)(2,1)S(1)}, bf16[64,4096]{1,0:T(8,128)(2,1)}, u32[]{:S(2)}) copy-start(bf16[64,4096]{1,0:T(8,128)(2,1)} %param.16) | copy-start | bytes 1572868
  48.8 0.7 copy-start.2
  48.8 29.3 %copy-start.13 = (s32[64,2]{0,1:T(2,128)S(1)}, s32[64,2]{0,1:T(2,128)}, u32[]{:S(2)}) copy-start(s32[64,2]{0,1:T(2,128)} %param.23) | copy-start | bytes 1540
  49.6 30.2 %collective-permute-start = (bf16[64,2048]{1,0:T(8,128)(2,1)}, bf16[64,2048]{1,0:T(8,128)(2,1)}, u32[]{:S(2)}, u32[]{:S(2)}) collective-permute-start(bf16[64,2048]{1,0:T(8,128)(2,1)} %param.21), channel_id=1, source_target_pairs={{0,2},{1,3},{2,4},{3,5},{4,6},{5,7},{6,8},{7,9},{8,10},{9,11},{10,... | collective-permute-start | bytes 786440 | tf_op jit(solution)/shard_map/ppermute | solution.py:31
  52.8 28.1 %collective-permute-start.1 = (bf16[64,2048]{1,0:T(8,128)(2,1)}, bf16[64,2048]{1,0:T(8,128)(2,1)}, u32[]{:S(2)}, u32[]{:S(2)}) collective-permute-start(bf16[64,2048]{1,0:T(8,128)(2,1)} %param.21), channel_id=1, source_target_pairs={{0,1},{1,2},{2,3},{3,4},{4,5},{5,6},{6,7},{7,8},{8,9},{9,10},{10,1... | collective-permute-start | bytes 786440 | tf_op jit(solution)/shard_map/ppermute | solution.py:31
  58.6 19.9 %copy-start.8 = (bf16[64,4096]{1,0:T(8,128)(2,1)S(1)}, bf16[64,4096]{1,0:T(8,128)(2,1)}, u32[]{:S(2)}) copy-start(bf16[64,4096]{1,0:T(8,128)(2,1)} %param.20) | copy-start | bytes 1572868
  80.8 3.7 %copy-start.9 = (bf16[64,8,4,128]{3,2,1,0:T(4,128)(2,1)S(1)}, bf16[64,8,4,128]{3,2,1,0:T(4,128)(2,1)}, u32[]{:S(2)}) copy-start(bf16[64,8,4,128]{3,2,1,0:T(4,128)(2,1)} %reshape.321) | copy-start | bytes 1572868
  102.8 3.1 %copy-start.6 = (f32[64,4096]{1,0:T(8,128)S(1)}, f32[64,4096]{1,0:T(8,128)}, u32[]{:S(2)}) copy-start(f32[64,4096]{1,0:T(8,128)} %reduce_window_sum.33) | copy-start | bytes 3145732
  105.9 5.4 %copy-start.7 = (f32[8,8,4096]{2,1,0:T(8,128)S(1)}, f32[8,8,4096]{2,1,0:T(8,128)}, u32[]{:S(2)}) copy-start(f32[8,8,4096]{2,1,0:T(8,128)} %get-tuple-element.46) | copy-start | bytes 3145732
  111.3 1.0 copy-start.5
  111.3 1.4 copy-start.10
  111.4 1.8 copy-start.4
  179.9 5.0 %copy-start.14 = (f32[64,2]{0,1:T(2,128)S(1)}, f32[64,2]{0,1:T(2,128)}, u32[]{:S(2)}) copy-start(f32[64,2]{0,1:T(2,128)} %param.24) | copy-start | bytes 1540
  179.9 52.6 %all-to-all-start.1 = ((bf16[16,12,4096]{2,1,0:T(8,128)(2,1)}), bf16[16,12,4096]{2,1,0:T(8,128)(2,1)}, u32[]{:S(2)}, u32[]{:S(2)}) async-start(bf16[16,12,4096]{2,1,0:T(8,128)(2,1)} %reshape.324), calls=%async_computation.1 | async-start | bytes 4194304 | tf_op jit(solution)/shard_map/all_to_all | solution.py:147
Sparse Core Ops, SparseCore 0:
  49.7 53.0 all-gather.3
where the time goes:
time: 244 us; the launch traced here: 243 us
  blocking collectives  69.9 us (29%)
  waiting for transfers between devices  58.7 us (24%)
  local copies, waits for them, and re-layouts  44.3 us (18%)
  other arithmetic  27.3 us (11%)
  matrix products  15.4 us (6%)
  between operations  14.4 us (6%)
  starting transfers between devices  12.2 us (5%)
    all_to_all x1, blocking collectives, body(): lax.all_to_all(outgoing, 'seq', split_axis=0, concat_axis=0, tiled=True)  51.8 us
    all_to_all x1, waiting for transfers between devices, body(): lax.all_to_all(partial_value.reshape(arrived.shape), 'seq', split_axis=0,...  47.5 us
    slice x8, local copies, waits for them, and re-layouts, sweep(): lax.scan(advance, initial, (values, deltas, inject_rows.T, read_rows.T),...  19.2 us
    all_gather x1, blocking collectives, ssm_correct(): sums = lax.all_gather(running[-1], 'seq')  18.1 us
    all_gather x1, waiting for transfers between devices, ssm_correct(): ends = lax.all_gather(local_end, 'seq')  11.2 us
    reduce_sum x24, other arithmetic, advance(): return (carried, jnp.sum(read_row[:, None] * carried, axis=0))  9.28 us
    ppermute x2, starting transfers between devices, shifted(): return lax.ppermute(value, axis, pairs)  7.14 us
    unnamed x36, local copies, waits for them, and re-layouts  6.72 us
  transfers between devices with their start and end apart: 4, of which 2 were waited for; matrix products, arithmetic and copies ran while one was open for 7% of the time, Pallas kernels for 0%

commit v1 on v0

--- a/solution.py
+++ b/solution.py
@@ -9,6 +9,17 @@
 HEAD_SIZE = 128
 EXP_WIN = 4
 CAP = 12
+
+
+def split_up(array, dim, size):
+    before, after = (array.shape[:dim], array.shape[dim + 1 :])
+    return jnp.moveaxis(array.reshape(*before, size, -1, *after), dim, 0)
+
+
+def in_order(pieces, dim):
+    shape = list(pieces.shape[1:])
+    shape[dim] *= pieces.shape[0]
+    return jnp.moveaxis(pieces, 0, dim).reshape(shape)
 
 
 def prefix(value, axis, join, neutral):
@@ -141,7 +152,14 @@
         "tek,td->ekd", picker.astype(jnp.bfloat16), stream, preferred_element_type=jnp.float32
     ).astype(jnp.bfloat16)
     outgoing = jnp.repeat(packed, group, axis=0)
-    arrived = lax.all_to_all(outgoing, "seq", split_axis=0, concat_axis=0, tiled=True)
+    peers, index = (lax.axis_size("seq"), lax.axis_index("seq"))
+    parts = split_up(outgoing, 0, peers)
+    finished = [parts[index]]
+    for step in range(1, peers):
+        sent = parts[index ^ step]
+        finished.append(lax.ppermute(sent, "seq", [(i_2, i_2 ^ step) for i_2 in range(peers)]))
+    parts = jnp.stack(finished)[index ^ jnp.arange(peers)]
+    arrived = in_order(parts, 0)
     gathered = arrived.reshape(-1, arrived.shape[-1])
     partial_value = expert_partial(gathered, w_gate, w_up, w_down)
     returned = lax.all_to_all(

time: 244 us -> 254 us (1.041)
  blocking collectives: 69.9 us -> 18.4 us
  waiting for transfers between devices: 58.7 us -> 87.9 us
  starting transfers between devices: 12.2 us -> 32.8 us
  local copies, waits for them, and re-layouts: 44.3 us -> 55.9 us
    all_to_all x1 -> x0, blocking collectives: 51.8 us -> none  [body(): lax.all_to_all(outgoing, 'seq', split_axis=0, concat_axis=0, tiled=True)]
    ppermute x0 -> x15, waiting for transfers between devices: none -> 26.9 us  [body(): lax.ppermute(sent, 'seq', [(i_2, i_2 ^ step) for i_2 in range(peers)])]
    ppermute x0 -> x15, starting transfers between devices: none -> 20.9 us  [body(): lax.ppermute(sent, 'seq', [(i_2, i_2 ^ step) for i_2 in range(peers)])]
    unnamed x36 -> x48, local copies, waits for them, and re-layouts: 6.72 us -> 14.7 us
    another operation x0 -> x2, local copies, waits for them, and re-layouts: none -> 4.23 us  [the longest x1 3.57 us: body(): gathered = arrived.reshape(-1, arrived.shape[-1])]
    gather x0 -> x1, local copies, waits for them, and re-layouts: none -> 3.62 us  [body(): parts = jnp.stack(finished)[index ^ jnp.arange(peers)]]
    reshape x1 -> x0, local copies, waits for them, and re-layouts: 3.57 us -> none  [body(): gathered = arrived.reshape(-1, arrived.shape[-1])]
  transfers between devices with their start and end apart: 4 -> 19, of which waited for: 2 -> 9; matrix products, arithmetic and copies ran while one was open for 7% -> 9% of each run, Pallas kernels for 0% -> 0%
where the time goes in v1:
time: 254 us; the launch traced here: 253 us
  waiting for transfers between devices  87.9 us (35%)
  local copies, waits for them, and re-layouts  55.9 us (22%)
  starting transfers between devices  32.8 us (13%)
  other arithmetic  28 us (11%)
  blocking collectives  18.4 us (7%)
  between operations  14.5 us (6%)
  matrix products  14.4 us (6%)
    all_to_all x1, waiting for transfers between devices, body(): lax.all_to_all(partial_value.reshape(arrived.shape), 'seq', split_axis=0,...  47.5 us
    ppermute x15, waiting for transfers between devices, body(): lax.ppermute(sent, 'seq', [(i_2, i_2 ^ step) for i_2 in range(peers)])  26.9 us
    ppermute x15, starting transfers between devices, body(): lax.ppermute(sent, 'seq', [(i_2, i_2 ^ step) for i_2 in range(peers)])  20.9 us
    slice x8, local copies, waits for them, and re-layouts, sweep(): lax.scan(advance, initial, (values, deltas, inject_rows.T, read_rows.T),...  19.2 us
    all_gather x1, blocking collectives, ssm_correct(): sums = lax.all_gather(running[-1], 'seq')  18.4 us
    unnamed x48, local copies, waits for them, and re-layouts  14.7 us
    all_gather x1, waiting for transfers between devices, ssm_correct(): ends = lax.all_gather(local_end, 'seq')  13.4 us
    reduce_sum x24, other arithmetic, advance(): return (carried, jnp.sum(read_row[:, None] * carried, axis=0))  9.28 us
  transfers between devices with their start and end apart: 19, of which 9 were waited for; matrix products, arithmetic and copies ran while one was open for 9% of the time, Pallas kernels for 0%

profile of v1, /device:TPU:11, one launch (start us, length us, event | category | flops | bytes accessed | tf_op | source)
XLA Modules:
  0.0 253.0 jit_solution(14934170155431126309)
XLA Ops:
  7.3 2.2 convert_bitcast_fusion
  9.5 2.1 bitcast_convert_fusion
  11.9 37.0 %while.13 = (s32[]{:T(128)}, f32[16,4096]{1,0:T(8,128)S(1)}, f32[8,8,4096]{2,1,0:T(8,128)}, f32[8,8,4096]{2,1,0:T(8,128)}, f32[16,4096]{1,0:T(8,128)S(1)}, /*ind...) while((s32[]{:T(128)}, f32[16,4096]{1,0:T(8,128)S(1)}, ...), condition=%wide.region_9.10_spmd.clone, body=%wide.region_0.9_spmd.clone.sunk | while | flops 4587530 | bytes 5150316 | solution.py:55
  16.2 2.6 %constant_dynamic-slice_fusion.21 = (f32[1,1,4096]{2,1,0:T(1,128)S(1)}, f32[1,1,4096]{2,1,0:T(1,128)S(1)}, f32[1,1,4096]{2,1,0:T(1,128)S(1)}, f32[1,1,4096]{2,1,...) fusion(f32[8,8,4096]{2,1,0:T(8,128)} %get-tuple-element.346, ...), kind=kLoop, calls=%fused_computation.25.clone.1 | loop fusion | bytes 524320 | tf_op jit(solution)/shard_map/while/body/slice | solution.py:55
  21.1 2.3 constant_dynamic-slice_fusion.21
  25.6 2.3 constant_dynamic-slice_fusion.21
  30.2 2.6 %constant_dynamic-slice_fusion.21 = (f32[1,1,4096]{2,1,0:T(1,128)S(1)}, f32[1,1,4096]{2,1,0:T(1,128)S(1)}, f32[1,1,4096]{2,1,0:T(1,128)S(1)}, f32[1,1,4096]{2,1,...) fusion(f32[8,8,4096]{2,1,0:T(8,128)} %get-tuple-element.346, ...), kind=kLoop, calls=%fused_computation.25.clone.1 | loop fusion | bytes 524320 | tf_op jit(solution)/shard_map/while/body/slice | solution.py:55
  35.0 2.3 constant_dynamic-slice_fusion.21
  39.5 2.4 constant_dynamic-slice_fusion.21
  44.1 2.5 %constant_dynamic-slice_fusion.21 = (f32[1,1,4096]{2,1,0:T(1,128)S(1)}, f32[1,1,4096]{2,1,0:T(1,128)S(1)}, f32[1,1,4096]{2,1,0:T(1,128)S(1)}, f32[1,1,4096]{2,1,...) fusion(f32[8,8,4096]{2,1,0:T(8,128)} %get-tuple-element.346, ...), kind=kLoop, calls=%fused_computation.25.clone.1 | loop fusion | bytes 524320 | tf_op jit(solution)/shard_map/while/body/slice | solution.py:55
  49.6 3.2 %collective-permute-start = (bf16[64,2048]{1,0:T(8,128)(2,1)}, bf16[64,2048]{1,0:T(8,128)(2,1)}, u32[]{:S(2)}, u32[]{:S(2)}) collective-permute-start(bf16[64,2048]{1,0:T(8,128)(2,1)} %param.21), channel_id=1, source_target_pairs={{0,2},{1,3},{2,4},{3,5},{4,6},{5,7},{6,8},{7,9},{8,10},{9,11},{10,... | collective-permute-start | bytes 786440 | tf_op jit(solution)/shard_map/ppermute | solution.py:42
  52.8 4.0 %collective-permute-start.1 = (bf16[64,2048]{1,0:T(8,128)(2,1)}, bf16[64,2048]{1,0:T(8,128)(2,1)}, u32[]{:S(2)}, u32[]{:S(2)}) collective-permute-start(bf16[64,2048]{1,0:T(8,128)(2,1)} %param.21), channel_id=1, source_target_pairs={{0,1},{1,2},{2,3},{3,4},{4,5},{5,6},{6,7},{7,8},{8,9},{9,10},{10,1... | collective-permute-start | bytes 786440 | tf_op jit(solution)/shard_map/ppermute | solution.py:42
  59.6 18.4 %all-gather.1 = f32[16,1,4096]{2,1,0:T(1,128)S(1)} all-gather(f32[1,1,4096]{2,1,0:T(1,128)S(1)} %slice_bitcast_fusion.18), channel_id=1, replica_groups=mesh['grp'=2,'seq'=16] {'seq'}, dimensions={0}, use_global_device_ids=true | all-gather | bytes 278528 | tf_op jit(solution)/shard_map/all_gather | solution.py:62
  84.0 2.3 fusion.51
  86.3 2.3 fusion.4
  89.4 13.4 %all-gather.4.cloned.1.call-done = f32[256,4096]{1,0:T(8,128)} async-done(((f32[16,4096]{1,0:T(8,128)}), f32[256,4096]{1,0:T(8,128)}) %all-gather.4.cloned.1.call-update) | async-done | bytes 4194320 | tf_op jit(solution)/shard_map/all_gather | solution.py:61
  102.8 3.1 %select_reduce_fusion = f32[16,4096]{1,0:T(8,128)S(1)} fusion(f32[16,16,4096]{2,1,0:T(8,128)} %bitcast.246, f32[16,4096]{1,0:T(8,128)} %subtract_maximum_fusion, f32[16,4096]{1,0:T(8,128)S(1)} %get-tuple-element.359, pred[16]{0:T(512)(128)(4,1)S(1)} %iota_compare_fusion.2), kind=kLoop, calls=%fused_computation.60 | loop fusion | flops 4128768 | bytes 4980752 | tf_op jit(solution)/shard_map/reduce_sum | solution.py:69
  106.0 5.3 %multiply_reduce_fusion.8 = f32[64,4096]{1,0:T(8,128)S(1)} fusion(f32[16,4096]{1,0:T(8,128)S(1)} %select_reduce_fusion, f32[64,4096]{1,0:T(8,128)S(1)} %copy-done.6, f32[16,4096]{1,0:T(8,128)S(1)} %get-tuple-element.359, f32[64,16]{1,0:T(8,128)S(1)} %bitcast.272), kind=kLoop, calls=%fused_computation.54 | loop fusion | flops 16515072 | bytes 2625536 | tf_op jit(solution)/shard_map/reduce_sum | solution.py:71
  119.5 2.3 collective-permute-start.8
  129.4 5.2 %collective-permute-start.12 = (bf16[1,12,4096]{2,1,0:T(8,128)(2,1)S(1)}, bf16[1,12,4096]{2,1,0:T(8,128)(2,1)S(1)}, u32[]{:S(2)}, u32[]{:S(2)}) collective-permute-start(bf16[1,12,4096]{2,1,0:T(8,128)(2,1)S(1)} %get-tuple-element.150), channel_id=1, source_target_pairs={{0,11},{1,10},{2,9},{3,8},{4,15},{5,14},{6,13},{7,12},{8,3},{9,2},... | collective-permute-start | bytes 294920 | tf_op jit(solution)/shard_map/ppermute | solution.py:160
  139.9 9.2 %collective-permute-done.11 = bf16[1,12,4096]{2,1,0:T(8,128)(2,1)S(1)} collective-permute-done((bf16[1,12,4096]{2,1,0:T(8,128)(2,1)S(1)}, bf16[1,12,4096]{2,1,0:T(8,128)(2,1)S(1)}, u32[]{:S(2)}, u32[]{:S(2)}) %collective-permute-start.11) | collective-permute-done | bytes 98336 | tf_op jit(solution)/shard_map/ppermute | solution.py:160
  151.8 2.8 %collective-permute-done.12 = bf16[1,12,4096]{2,1,0:T(8,128)(2,1)S(1)} collective-permute-done((bf16[1,12,4096]{2,1,0:T(8,128)(2,1)S(1)}, bf16[1,12,4096]{2,1,0:T(8,128)(2,1)S(1)}, u32[]{:S(2)}, u32[]{:S(2)}) %collective-permute-start.12) | collective-permute-done | bytes 98336 | tf_op jit(solution)/shard_map/ppermute | solution.py:160
  155.2 6.6 %collective-permute-done.13 = bf16[1,12,4096]{2,1,0:T(8,128)(2,1)S(1)} collective-permute-done((bf16[1,12,4096]{2,1,0:T(8,128)(2,1)S(1)}, bf16[1,12,4096]{2,1,0:T(8,128)(2,1)S(1)}, u32[]{:S(2)}, u32[]{:S(2)}) %collective-permute-start.13) | collective-permute-done | bytes 98336 | tf_op jit(solution)/shard_map/ppermute | solution.py:160
  165.2 2.9 %collective-permute-done.15 = bf16[1,12,4096]{2,1,0:T(8,128)(2,1)S(1)} collective-permute-done((bf16[1,12,4096]{2,1,0:T(8,128)(2,1)S(1)}, bf16[1,12,4096]{2,1,0:T(8,128)(2,1)S(1)}, u32[]{:S(2)}, u32[]{:S(2)}) %collective-permute-start.15) | collective-permute-done | bytes 98336 | tf_op jit(solution)/shard_map/ppermute | solution.py:160
  168.7 2.2 collective-permute-done.16
  171.6 3.6 %gather_fusion = bf16[16,12,4096]{2,1,0:T(8,128)(2,1)} fusion(bf16[16,12,4096]{2,1,0:T(8,128)(2,1)} %bitcast.45, s32[1024]{0:T(1024)S(1)} %pad_clamp_fusion), kind=kCustom, calls=%fused_computation | custom fusion | bytes 3145792 | tf_op jit(solution)/shard_map/gather | solution.py:161
  175.2 3.6 %reshape_reshape.7 = bf16[192,4096]{1,0:T(8,128)(2,1)} reshape(bf16[16,12,4096]{2,1,0:T(8,128)(2,1)} %gather_fusion) | data formatting | bytes 3145728 | tf_op jit(solution)/shard_map/reshape;reshape | solution.py:163
  178.7 2.6 %fusion.56 = f32[192,256]{1,0:T(8,128)S(1)} fusion(bf16[192,4096]{1,0:T(8,128)(2,1)} %reshape_reshape.7, bf16[4096,256]{1,0:T(8,128)(2,1)} %param.25), kind=kOutput, calls=%fused_computation.155 | convolution fusion | flops 402653184 | bytes 3866624 | tf_op jit(solution)/shard_map/dot_general | solution.py:101
  181.4 5.1 %convolution_convert_fusion = bf16[192,4096]{1,0:T(8,128)(2,1)} fusion(bf16[256,4096]{1,0:T(8,128)(2,1)S(1)} %copy-done, bf16[192,4096]{1,0:T(8,128)(2,1)} %reshape_reshape.7, bf16[4096,256]{1,0:T(8,128)(2,1)} %param.26, f32[192,256]{1,0:T(8,128)S(1)} %fusion.56), kind=kOutput, calls=%fused_computation.55 | convolution fusion | flops 806387712 | bytes 7536640 | tf_op jit(solution)/shard_map/dot_general | solution.py:104
  186.5 3.4 %reshape.332 = bf16[16,12,4096]{2,1,0:T(8,128)(2,1)} reshape(bf16[192,4096]{1,0:T(8,128)(2,1)} %convolution_convert_fusion) | data formatting | bytes 3145728 | tf_op jit(solution)/shard_map/reshape | solution.py:166
  189.9 4.7 %all-to-all-start = ((bf16[16,12,4096]{2,1,0:T(8,128)(2,1)}), bf16[16,12,4096]{2,1,0:T(8,128)(2,1)}, u32[]{:S(2)}, u32[]{:S(2)}) async-start(bf16[16,12,4096]{2,1,0:T(8,128)(2,1)} %reshape.332), calls=%async_computation | async-start | bytes 4194304 | tf_op jit(solution)/shard_map/all_to_all | solution.py:165
  194.7 47.5 %all-to-all-done = bf16[16,12,4096]{2,1,0:T(8,128)(2,1)} async-done(((bf16[16,12,4096]{2,1,0:T(8,128)(2,1)}), bf16[16,12,4096]{2,1,0:T(8,128)(2,1)}, u32[]{:S(2)}, u32[]{:S(2)}) %all-to-all-start) | async-done | bytes 1572896 | tf_op jit(solution)/shard_map/all_to_all | solution.py:165
  (245 shorter events, 62.4 us)
Async XLA Ops:
  7.2 174.2 %copy-start = (bf16[256,4096]{1,0:T(8,128)(2,1)S(1)}, bf16[256,4096]{1,0:T(8,128)(2,1)}, u32[]{:S(2)}) copy-start(bf16[256,4096]{1,0:T(8,128)(2,1)} %param.27) | copy-start | bytes 6291460
  7.2 4.5 %copy-start.10 = (f32[16,64]{1,0:T(8,128)S(1)}, f32[16,64]{1,0:T(8,128)}, u32[]{:S(2)}) copy-start(f32[16,64]{1,0:T(8,128)} %param.18) | copy-start | bytes 12292
  7.2 4.6 %copy-start.11 = (f32[16,64]{1,0:T(8,128)S(1)}, f32[16,64]{1,0:T(8,128)}, u32[]{:S(2)}) copy-start(f32[16,64]{1,0:T(8,128)} %param.19) | copy-start | bytes 12292
  7.2 4.6 %copy-start.1 = (f32[16,4096]{1,0:T(8,128)S(1)}, f32[16,4096]{1,0:T(8,128)}, u32[]{:S(2)}) copy-start(f32[16,4096]{1,0:T(8,128)} %param.17) | copy-start | bytes 786436
  7.2 95.6 %all-gather.4.cloned.1.call-start = ((), (), s32[]{:S(2)}) async-start(), calls=%async_computation.1 | async-start | bytes 4456448 | tf_op jit(solution)/shard_map/all_gather | solution.py:61
  11.8 44.9 %copy-start.3 = (bf16[64,4096]{1,0:T(8,128)(2,1)S(1)}, bf16[64,4096]{1,0:T(8,128)(2,1)}, u32[]{:S(2)}) copy-start(bf16[64,4096]{1,0:T(8,128)(2,1)} %param.16) | copy-start | bytes 1572868
  48.8 29.6 %copy-start.12 = (s32[64,2]{0,1:T(2,128)S(1)}, s32[64,2]{0,1:T(2,128)}, u32[]{:S(2)}) copy-start(s32[64,2]{0,1:T(2,128)} %param.23) | copy-start | bytes 1540
  49.6 30.6 %collective-permute-start = (bf16[64,2048]{1,0:T(8,128)(2,1)}, bf16[64,2048]{1,0:T(8,128)(2,1)}, u32[]{:S(2)}, u32[]{:S(2)}) collective-permute-start(bf16[64,2048]{1,0:T(8,128)(2,1)} %param.21), channel_id=1, source_target_pairs={{0,2},{1,3},{2,4},{3,5},{4,6},{5,7},{6,8},{7,9},{8,10},{9,11},{10,... | collective-permute-start | bytes 786440 | tf_op jit(solution)/shard_map/ppermute | solution.py:42
  52.8 28.4 %collective-permute-start.1 = (bf16[64,2048]{1,0:T(8,128)(2,1)}, bf16[64,2048]{1,0:T(8,128)(2,1)}, u32[]{:S(2)}, u32[]{:S(2)}) collective-permute-start(bf16[64,2048]{1,0:T(8,128)(2,1)} %param.21), channel_id=1, source_target_pairs={{0,1},{1,2},{2,3},{3,4},{4,5},{5,6},{6,7},{7,8},{8,9},{9,10},{10,1... | collective-permute-start | bytes 786440 | tf_op jit(solution)/shard_map/ppermute | solution.py:42
  58.6 21.0 %copy-start.8 = (bf16[64,4096]{1,0:T(8,128)(2,1)S(1)}, bf16[64,4096]{1,0:T(8,128)(2,1)}, u32[]{:S(2)}) copy-start(bf16[64,4096]{1,0:T(8,128)(2,1)} %param.20) | copy-start | bytes 1572868
  89.3 22.1 %copy-start.5 = (bf16[64,4096]{1,0:T(8,128)(2,1)}, bf16[64,4096]{1,0:T(8,128)(2,1)S(1)}, u32[]{:S(2)}) copy-start(bf16[64,4096]{1,0:T(8,128)(2,1)S(1)} %convert_element_type.67) | copy-start | bytes 1572868
  102.8 3.1 %copy-start.6 = (f32[64,4096]{1,0:T(8,128)S(1)}, f32[64,4096]{1,0:T(8,128)}, u32[]{:S(2)}) copy-start(f32[64,4096]{1,0:T(8,128)} %reduce_window_sum.33) | copy-start | bytes 3145732
  105.9 5.4 %copy-start.7 = (f32[8,8,4096]{2,1,0:T(8,128)S(1)}, f32[8,8,4096]{2,1,0:T(8,128)}, u32[]{:S(2)}) copy-start(f32[8,8,4096]{2,1,0:T(8,128)} %get-tuple-element.46) | copy-start | bytes 3145732
  111.3 1.1 copy-start.9
  111.4 1.5 copy-start.4
  113.9 3.8 %collective-permute-start.2 = (bf16[1,12,4096]{2,1,0:T(8,128)(2,1)S(1)}, bf16[1,12,4096]{2,1,0:T(8,128)(2,1)S(1)}, u32[]{:S(2)}, u32[]{:S(2)}) collective-permute-start(bf16[1,12,4096]{2,1,0:T(8,128)(2,1)S(1)} %get-tuple-element.160), channel_id=1, source_target_pairs={{0,1},{1,0},{2,3},{3,2},{4,5},{5,4},{6,7},{7,6},{8,9},{9,8},{10,11... | collective-permute-start | bytes 294920 | tf_op jit(solution)/shard_map/ppermute | solution.py:160
  114.2 5.3 %collective-permute-start.3 = (bf16[1,12,4096]{2,1,0:T(8,128)(2,1)S(1)}, bf16[1,12,4096]{2,1,0:T(8,128)(2,1)S(1)}, u32[]{:S(2)}, u32[]{:S(2)}) collective-permute-start(bf16[1,12,4096]{2,1,0:T(8,128)(2,1)S(1)} %get-tuple-element.159), channel_id=1, source_target_pairs={{0,2},{1,3},{2,0},{3,1},{4,6},{5,7},{6,4},{7,5},{8,10},{9,11},{10,... | collective-permute-start | bytes 294920 | tf_op jit(solution)/shard_map/ppermute | solution.py:160
  115.3 7.1 %collective-permute-start.4 = (bf16[1,12,4096]{2,1,0:T(8,128)(2,1)S(1)}, bf16[1,12,4096]{2,1,0:T(8,128)(2,1)S(1)}, u32[]{:S(2)}, u32[]{:S(2)}) collective-permute-start(bf16[1,12,4096]{2,1,0:T(8,128)(2,1)S(1)} %get-tuple-element.158), channel_id=1, source_target_pairs={{0,3},{1,2},{2,1},{3,0},{4,7},{5,6},{6,5},{7,4},{8,11},{9,10},{10,... | collective-permute-start | bytes 294920 | tf_op jit(solution)/shard_map/ppermute | solution.py:160
  116.1 8.6 %collective-permute-start.5 = (bf16[1,12,4096]{2,1,0:T(8,128)(2,1)S(1)}, bf16[1,12,4096]{2,1,0:T(8,128)(2,1)S(1)}, u32[]{:S(2)}, u32[]{:S(2)}) collective-permute-start(bf16[1,12,4096]{2,1,0:T(8,128)(2,1)S(1)} %get-tuple-element.157), channel_id=1, source_target_pairs={{0,4},{1,5},{2,6},{3,7},{4,0},{5,1},{6,2},{7,3},{8,12},{9,13},{10,... | collective-permute-start | bytes 294920 | tf_op jit(solution)/shard_map/ppermute | solution.py:160
  116.3 9.7 %collective-permute-start.6 = (bf16[1,12,4096]{2,1,0:T(8,128)(2,1)S(1)}, bf16[1,12,4096]{2,1,0:T(8,128)(2,1)S(1)}, u32[]{:S(2)}, u32[]{:S(2)}) collective-permute-start(bf16[1,12,4096]{2,1,0:T(8,128)(2,1)S(1)} %get-tuple-element.156), channel_id=1, source_target_pairs={{0,5},{1,4},{2,7},{3,6},{4,1},{5,0},{6,3},{7,2},{8,13},{9,12},{10,... | collective-permute-start | bytes 294920 | tf_op jit(solution)/shard_map/ppermute | solution.py:160
  117.7 11.8 %collective-permute-start.7 = (bf16[1,12,4096]{2,1,0:T(8,128)(2,1)S(1)}, bf16[1,12,4096]{2,1,0:T(8,128)(2,1)S(1)}, u32[]{:S(2)}, u32[]{:S(2)}) collective-permute-start(bf16[1,12,4096]{2,1,0:T(8,128)(2,1)S(1)} %get-tuple-element.155), channel_id=1, source_target_pairs={{0,6},{1,7},{2,4},{3,5},{4,2},{5,3},{6,0},{7,1},{8,14},{9,15},{10,... | collective-permute-start | bytes 294920 | tf_op jit(solution)/shard_map/ppermute | solution.py:160
  119.5 15.8 %collective-permute-start.8 = (bf16[1,12,4096]{2,1,0:T(8,128)(2,1)S(1)}, bf16[1,12,4096]{2,1,0:T(8,128)(2,1)S(1)}, u32[]{:S(2)}, u32[]{:S(2)}) collective-permute-start(bf16[1,12,4096]{2,1,0:T(8,128)(2,1)S(1)} %get-tuple-element.154), channel_id=1, source_target_pairs={{0,7},{1,6},{2,5},{3,4},{4,3},{5,2},{6,1},{7,0},{8,15},{9,14},{10,... | collective-permute-start | bytes 294920 | tf_op jit(solution)/shard_map/ppermute | solution.py:160
  122.5 14.0 %collective-permute-start.9 = (bf16[1,12,4096]{2,1,0:T(8,128)(2,1)S(1)}, bf16[1,12,4096]{2,1,0:T(8,128)(2,1)S(1)}, u32[]{:S(2)}, u32[]{:S(2)}) collective-permute-start(bf16[1,12,4096]{2,1,0:T(8,128)(2,1)S(1)} %get-tuple-element.153), channel_id=1, source_target_pairs={{0,8},{1,9},{2,10},{3,11},{4,12},{5,13},{6,14},{7,15},{8,0},{9,1},... | collective-permute-start | bytes 294920 | tf_op jit(solution)/shard_map/ppermute | solution.py:160
  124.6 13.0 %collective-permute-start.10 = (bf16[1,12,4096]{2,1,0:T(8,128)(2,1)S(1)}, bf16[1,12,4096]{2,1,0:T(8,128)(2,1)S(1)}, u32[]{:S(2)}, u32[]{:S(2)}) collective-permute-start(bf16[1,12,4096]{2,1,0:T(8,128)(2,1)S(1)} %get-tuple-element.152), channel_id=1, source_target_pairs={{0,9},{1,8},{2,11},{3,10},{4,13},{5,12},{6,15},{7,14},{8,1},{9,0},... | collective-permute-start | bytes 294920 | tf_op jit(solution)/shard_map/ppermute | solution.py:160
  126.0 23.0 %collective-permute-start.11 = (bf16[1,12,4096]{2,1,0:T(8,128)(2,1)S(1)}, bf16[1,12,4096]{2,1,0:T(8,128)(2,1)S(1)}, u32[]{:S(2)}, u32[]{:S(2)}) collective-permute-start(bf16[1,12,4096]{2,1,0:T(8,128)(2,1)S(1)} %get-tuple-element.151), channel_id=1, source_target_pairs={{0,10},{1,11},{2,8},{3,9},{4,14},{5,15},{6,12},{7,13},{8,2},{9,3},... | collective-permute-start | bytes 294920 | tf_op jit(solution)/shard_map/ppermute | solution.py:160
  129.4 25.1 %collective-permute-start.12 = (bf16[1,12,4096]{2,1,0:T(8,128)(2,1)S(1)}, bf16[1,12,4096]{2,1,0:T(8,128)(2,1)S(1)}, u32[]{:S(2)}, u32[]{:S(2)}) collective-permute-start(bf16[1,12,4096]{2,1,0:T(8,128)(2,1)S(1)} %get-tuple-element.150), channel_id=1, source_target_pairs={{0,11},{1,10},{2,9},{3,8},{4,15},{5,14},{6,13},{7,12},{8,3},{9,2},... | collective-permute-start | bytes 294920 | tf_op jit(solution)/shard_map/ppermute | solution.py:160
  135.2 26.6 %collective-permute-start.13 = (bf16[1,12,4096]{2,1,0:T(8,128)(2,1)S(1)}, bf16[1,12,4096]{2,1,0:T(8,128)(2,1)S(1)}, u32[]{:S(2)}, u32[]{:S(2)}) collective-permute-start(bf16[1,12,4096]{2,1,0:T(8,128)(2,1)S(1)} %get-tuple-element.149), channel_id=1, source_target_pairs={{0,12},{1,13},{2,14},{3,15},{4,8},{5,9},{6,10},{7,11},{8,4},{9,5},... | collective-permute-start | bytes 294920 | tf_op jit(solution)/shard_map/ppermute | solution.py:160
  136.5 28.0 %collective-permute-start.14 = (bf16[1,12,4096]{2,1,0:T(8,128)(2,1)S(1)}, bf16[1,12,4096]{2,1,0:T(8,128)(2,1)S(1)}, u32[]{:S(2)}, u32[]{:S(2)}) collective-permute-start(bf16[1,12,4096]{2,1,0:T(8,128)(2,1)S(1)} %get-tuple-element.148), channel_id=1, source_target_pairs={{0,13},{1,12},{2,15},{3,14},{4,9},{5,8},{6,11},{7,10},{8,5},{9,4},... | collective-permute-start | bytes 294920 | tf_op jit(solution)/shard_map/ppermute | solution.py:160
  137.6 30.5 %collective-permute-start.15 = (bf16[1,12,4096]{2,1,0:T(8,128)(2,1)S(1)}, bf16[1,12,4096]{2,1,0:T(8,128)(2,1)S(1)}, u32[]{:S(2)}, u32[]{:S(2)}) collective-permute-start(bf16[1,12,4096]{2,1,0:T(8,128)(2,1)S(1)} %get-tuple-element.147), channel_id=1, source_target_pairs={{0,14},{1,15},{2,12},{3,13},{4,10},{5,11},{6,8},{7,9},{8,6},{9,7},... | collective-permute-start | bytes 294920 | tf_op jit(solution)/shard_map/ppermute | solution.py:160
  149.1 21.8 %collective-permute-start.16 = (bf16[1,12,4096]{2,1,0:T(8,128)(2,1)S(1)}, bf16[1,12,4096]{2,1,0:T(8,128)(2,1)S(1)}, u32[]{:S(2)}, u32[]{:S(2)}) collective-permute-start(bf16[1,12,4096]{2,1,0:T(8,128)(2,1)S(1)} %get-tuple-element.146), channel_id=1, source_target_pairs={{0,15},{1,14},{2,13},{3,12},{4,11},{5,10},{6,9},{7,8},{8,7},{9,6},... | collective-permute-start | bytes 294920 | tf_op jit(solution)/shard_map/ppermute | solution.py:160
  189.9 4.7 %copy-start.13 = (f32[64,2]{0,1:T(2,128)S(1)}, f32[64,2]{0,1:T(2,128)}, u32[]{:S(2)}) copy-start(f32[64,2]{0,1:T(2,128)} %param.24) | copy-start | bytes 1540
  189.9 52.3 %all-to-all-start = ((bf16[16,12,4096]{2,1,0:T(8,128)(2,1)}), bf16[16,12,4096]{2,1,0:T(8,128)(2,1)}, u32[]{:S(2)}, u32[]{:S(2)}) async-start(bf16[16,12,4096]{2,1,0:T(8,128)(2,1)} %reshape.332), calls=%async_computation | async-start | bytes 4194304 | tf_op jit(solution)/shard_map/all_to_all | solution.py:165
  (1 other events, 0.7 us)
Sparse Core Ops, SparseCore 0:
  49.7 53.0 all-gather.3
